TPU v7x, 32 devices: a whole 2x2x4 slice. The times are simulated.
32 devices in a mesh: pair: 4 (over z), gen: 8 (over y, x, core).
Axes of the slice: x: 2, y: 2, z: 4, core: 2. Of those that a mesh axis runs over, the one named last changes fastest.
Arguments:
- tokens: bfloat16 [32768, 2048], P(('pair', 'gen')), may hold values from -6 to 6
- cotangent: bfloat16 [32768, 256], P(('pair', 'gen')), may hold values from -6 to 6
- block_pair: int32 [32, 1], replicated, may hold values from 0 to 15
- src_lang: int32 [16], replicated, may hold values from 0 to 95
- tgt_lang: int32 [16], replicated, may hold values from 0 to 95
- lang_embed: float32 [96, 512], P(None, 'pair'), may hold values from -5 to 5
- generator: bfloat16 [512, 524288], P('pair', 'gen'), may hold values from -0.005859375 to 0.005859375
Outputs:
- grad_tokens: bfloat16 [32768, 2048], P(('pair', 'gen'))
- grad_generator: bfloat16 [512, 524288], P('pair', 'gen')
- grad_embed: float32 [96, 512], P(None, 'pair')
Inputs may be any that keep to these rules, and one draw needn't show every extreme that they name: `block_pair`: every pair owns at least one block; block counts per pair are uneven.
All inputs are finite; a program needn't handle non-finite values.
Results may differ from a plain program's by a relative error of at most 0.007.
Values may be sent and summed in bfloat16 or wider, within the bound.
No kernel may reach another device: no remote copies, remote signals or barrier semaphores. Data moves between devices by JAX's collectives and lax.ppermute only.
A program may use at most 128 MiB of HBM per device.

v0:
```python
import jax
import jax.numpy as jnp
from jax import lax
from jax.sharding import PartitionSpec as P

BLK = 1024


def shards(tokens, cotangent, block_pair, src_lang, tgt_lang, lang_embed, generator):
    gen_count = lax.axis_size("gen")
    pair_index = lax.axis_index("pair")
    blocks_here = tokens.shape[0] // BLK
    model_width = tokens.shape[1]
    adapter_rank = cotangent.shape[1]
    languages = lang_embed.shape[0]
    pair_count = src_lang.shape[0]
    lang_ids = jnp.arange(languages, dtype=jnp.int32)
    hot_both = (src_lang[:, None] == lang_ids[None, :]).astype(jnp.float32) + (
        tgt_lang[:, None] == lang_ids[None, :]
    ).astype(jnp.float32)
    pair_embed = jnp.dot(hot_both, lang_embed, precision=lax.Precision.HIGHEST).astype(jnp.bfloat16)
    partial_value = jnp.dot(pair_embed, generator, preferred_element_type=jnp.float32)
    adapter_cols = lax.psum(partial_value, "pair").astype(jnp.bfloat16)
    flat_pairs = block_pair[:, 0]
    row_pairs = lax.dynamic_slice_in_dim(
        flat_pairs, pair_index * (gen_count * blocks_here), gen_count * blocks_here
    )
    send_order = row_pairs.reshape(gen_count, blocks_here).T
    outgoing = jnp.take(adapter_cols, send_order, axis=0).reshape(
        blocks_here, gen_count * adapter_cols.shape[1]
    )
    own_adapters = lax.all_to_all(outgoing, "gen", split_axis=1, concat_axis=1, tiled=True)
    adapters = own_adapters.reshape(blocks_here, model_width, adapter_rank)
    token_blocks = tokens.reshape(blocks_here, BLK, model_width)
    cot_blocks = cotangent.reshape(blocks_here, BLK, adapter_rank)
    hidden = jnp.einsum("btd,bdr->btr", token_blocks, adapters, preferred_element_type=jnp.float32)
    logistic = jax.nn.sigmoid(hidden)
    grad_hidden = (
        cot_blocks.astype(jnp.float32) * logistic * (1.0 + hidden * (1.0 - logistic))
    ).astype(jnp.bfloat16)
    grad_tokens = (
        jnp.einsum("btr,bdr->btd", grad_hidden, adapters, preferred_element_type=jnp.float32)
        .astype(jnp.bfloat16)
        .reshape(tokens.shape)
    )
    outer_grads = jnp.einsum(
        "btd,btr->bdr", token_blocks, grad_hidden, preferred_element_type=jnp.float32
    ).reshape(blocks_here, model_width * adapter_rank)
    returned = lax.all_to_all(outer_grads, "gen", split_axis=1, concat_axis=0, tiled=True)
    pair_ids = jnp.arange(pair_count, dtype=jnp.int32)
    segment_hot = (pair_ids[:, None] == row_pairs[None, :]).astype(jnp.float32)
    row_grad = jnp.dot(segment_hot, returned, precision=lax.Precision.HIGHEST)
    grad_rounded = lax.psum(row_grad, "pair").astype(jnp.bfloat16)
    grad_generator = jnp.einsum(
        "pe,pc->ec", pair_embed, grad_rounded, preferred_element_type=jnp.float32
    ).astype(jnp.bfloat16)
    partial_pair = jnp.einsum(
        "pc,ec->pe", grad_rounded, generator, preferred_element_type=jnp.float32
    )
    grad_pair = lax.psum(partial_pair, "gen")
    grad_embed = jnp.dot(hot_both.T, grad_pair, precision=lax.Precision.HIGHEST)
    return (grad_tokens, grad_generator, grad_embed)


def solution(mesh):
    placed = (
        P(("pair", "gen"), None),
        P(("pair", "gen"), None),
        P(),
        P(),
        P(),
        P(None, "pair"),
        P("pair", "gen"),
    )
    return jax.shard_map(
        shards,
        mesh=mesh,
        in_specs=placed,
        out_specs=(P(("pair", "gen"), None), P("pair", "gen"), P(None, "pair")),
        check_vma=False,
    )
```

profile of v0, /device:TPU:0, one launch (start us, length us, event | category | flops | bytes accessed | tf_op | source)
XLA Modules:
  0.0 421.6 jit_solution(15591775119214140472)
XLA Ops:
  3.0 10.1 %fusion.21 = f32[16,65536]{1,0:T(8,128)} fusion(bf16[16,128]{1,0:T(8,128)(2,1)S(1)} %convolution_convert_fusion.2, bf16[128,65536]{1,0:T(8,128)(2,1)} %param.13), kind=kOutput, calls=%fused_computation.39 | convolution fusion | flops 268435456 | bytes 20975616 | tf_op jit(solution)/shard_map/dot_general | solution.py:22
  13.1 149.0 %all-reduce.2 = bf16[16,65536]{1,0:T(8,128)(2,1)S(1)} all-reduce(f32[16,65536]{1,0:T(8,128)} %fusion.21), channel_id=1, replica_groups=mesh['pair'=4,'gen'=8] {'pair'}, use_global_device_ids=true, to_apply=%region_0.0 | all-reduce | flops 1048576 | bytes 6291456 | tf_op jit(solution)/shard_map/psum | solution.py:23
  162.1 1.2 gather_fusion
  163.5 1.6 copy.27
  165.7 7.0 %reduce.2 = bf16[8,65536]{1,0:T(8,128)(2,1)S(1)} reduce(bf16[8,1,65536]{2,1,0:T(2,128)(2,1)S(1)} %bitcast.33, bf16[]{:T(256)} %broadcast.100), dimensions={1}, to_apply=%bitcast.32.reduce_sub_computation | reduce | bytes 2097154
  172.7 1.9 reshape.166
  174.6 3.8 all-to-all-start
  178.4 1.0 copy.17
  179.4 14.3 %all-to-all-done = bf16[8,2,32768]{2,1,0:T(2,128)(2,1)S(1)} async-done(((bf16[8,2,32768]{2,1,0:T(2,128)(2,1)}), bf16[8,2,32768]{2,1,0:T(2,128)(2,1)S(1)}, u32[]{:S(2)}, u32[]{:S(2)}) %all-to-all-start) | async-done | bytes 1048608 | tf_op jit(solution)/shard_map/all_to_all | solution.py:32
  193.7 1.0 reshape.167
  194.8 6.0 %bitcast_reduce_fusion = bf16[8,65536]{1,0:T(8,128)(2,1)S(1)} fusion(bf16[8,1,65536]{2,1,0:T(2,128)(2,1)S(1)} %reshape.167), kind=kLoop, calls=%fused_computation.37 | loop fusion | bytes 2097152 | tf_op jit(solution)/shard_map/all_to_all | solution.py:32
  201.3 3.9 convolution_bitcast_fusion.1
  205.2 1.0 copy-done.9
  206.2 2.9 convolution_bitcast_fusion
  209.1 1.9 copy.19
  211.0 4.2 all_to_all.20
  215.2 3.9 all-to-all-start.1
  219.0 5.0 %convolution_convert_fusion.1 = bf16[1024,2048]{1,0:T(8,128)(2,1)} fusion(bf16[2048,256]{1,0:T(8,128)(2,1)S(1)} %copy-done.3, f32[1024,256]{0,1:T(8,128)} %copy-done.9, bf16[1024,256]{0,1:T(8,128)(2,1)} %copy.17), kind=kOutput, calls=%fused_computation.2 | convolution fusion | flops 1078460416 | bytes 6815744 | tf_op jit(solution)/shard_map/btr,bdr->btd/dot_general | solution.py:42
  224.0 21.3 %all-to-all-done.1 = f32[1,8,65536]{2,0,1:T(1,128)S(1)} async-done(((f32[1,8,65536]{2,0,1:T(1,128)}), f32[1,8,65536]{2,0,1:T(1,128)S(1)}, u32[]{:S(2)}, u32[]{:S(2)}) %all-to-all-start.1) | async-done | bytes 2097184 | tf_op jit(solution)/shard_map/all_to_all | solution.py:49
  245.3 4.8 %fusion = f32[16,65536]{1,0:T(8,128)} fusion(f32[1,8,65536]{2,0,1:T(1,128)S(1)} %all-to-all-done.1, s32[8]{0:T(128)S(1)} %get-tuple-element.4), kind=kOutput, calls=%fused_computation.4 | convolution fusion | flops 100663424 | bytes 6291488 | tf_op jit(solution)/shard_map/dot_general | solution.py:52
  250.1 141.2 %all-reduce.3 = bf16[16,65536]{1,0:T(8,128)(2,1)S(1)} all-reduce(f32[16,65536]{1,0:T(8,128)} %fusion), channel_id=1, replica_groups=mesh['pair'=4,'gen'=8] {'pair'}, use_global_device_ids=true, to_apply=%region_1.2 | all-reduce | flops 1048576 | bytes 6291456 | tf_op jit(solution)/shard_map/psum | solution.py:53
  391.4 8.5 %convolution_convert_fusion = bf16[128,65536]{1,0:T(8,128)(2,1)} fusion(bf16[16,128]{1,0:T(8,128)(2,1)S(1)} %convolution_convert_fusion.2, bf16[16,65536]{1,0:T(8,128)(2,1)S(1)} %all-reduce.3), kind=kOutput, calls=%fused_computation.1 | convolution fusion | flops 276824064 | bytes 18878464 | tf_op jit(solution)/shard_map/pe,pc->ec/dot_general | solution.py:54
  399.9 8.1 %fusion.22 = f32[16,128]{1,0:T(8,128)S(1)} fusion(bf16[16,65536]{1,0:T(8,128)(2,1)S(1)} %all-reduce.3, bf16[128,65536]{1,0:T(8,128)(2,1)} %param.13), kind=kOutput, calls=%fused_computation.40 | convolution fusion | flops 268435456 | bytes 18882560 | tf_op jit(solution)/shard_map/pc,ec->pe/dot_general | solution.py:57
  408.0 12.6 %psum.23 = f32[16,128]{1,0:T(8,128)S(1)} all-reduce(f32[16,128]{1,0:T(8,128)S(1)} %fusion.22), channel_id=1, replica_groups=mesh['pair'=4,'gen'=8] {'gen'}, use_global_device_ids=true, to_apply=%region_2.3 | all-reduce | flops 2048 | bytes 16384 | tf_op jit(solution)/shard_map/psum | solution.py:60
  (27 shorter events, 4.5 us)
Async XLA Ops:
  0.6 1.5 copy-start
  172.7 5.7 %copy-start.4 = (bf16[1024,256]{1,0:T(8,128)(2,1)S(1)}, bf16[1024,256]{1,0:T(8,128)(2,1)}, u32[]{:S(2)}) copy-start(bf16[1024,256]{1,0:T(8,128)(2,1)} %param.8) | copy-start | bytes 1572868
  174.6 19.1 %all-to-all-start = ((bf16[8,2,32768]{2,1,0:T(2,128)(2,1)}), bf16[8,2,32768]{2,1,0:T(2,128)(2,1)S(1)}, u32[]{:S(2)}, u32[]{:S(2)}) async-start(bf16[8,2,32768]{2,1,0:T(2,128)(2,1)} %reshape.166), calls=%async_computation | async-start | bytes 2097152 | tf_op jit(solution)/shard_map/all_to_all | solution.py:32
  201.3 3.9 copy-start.2
  201.3 4.9 %copy-start.5 = (bf16[1024,256]{0,1:T(8,128)(2,1)S(1)}, bf16[1024,256]{0,1:T(8,128)(2,1)}, u32[]{:S(2)}) copy-start(bf16[1024,256]{0,1:T(8,128)(2,1)} %copy.17) | copy-start | bytes 1572868
  201.3 4.9 %copy-start.6 = (bf16[1024,2048]{1,0:T(8,128)(2,1)S(1)}, bf16[1024,2048]{1,0:T(8,128)(2,1)}, u32[]{:S(2)}) copy-start(bf16[1024,2048]{1,0:T(8,128)(2,1)} %param.7) | copy-start | bytes 12582916
  205.2 1.0 copy-start.9
  211.0 8.0 %copy-start.3 = (bf16[2048,256]{1,0:T(8,128)(2,1)S(1)}, bf16[2048,256]{1,0:T(8,128)(2,1)}, u32[]{:S(2)}) copy-start(bf16[2048,256]{1,0:T(8,128)(2,1)} %copy-done.2) | copy-start | bytes 3145732
  215.2 30.2 %all-to-all-start.1 = ((f32[1,8,65536]{2,0,1:T(1,128)}), f32[1,8,65536]{2,0,1:T(1,128)S(1)}, u32[]{:S(2)}, u32[]{:S(2)}) async-start(f32[1,8,65536]{2,0,1:T(1,128)} %all_to_all.20), calls=%async_computation.1 | async-start | bytes 4194304 | tf_op jit(solution)/shard_map/all_to_all | solution.py:49
  399.9 20.7 %copy-start.7 = (s32[16]{0:T(128)S(1)}, s32[16]{0:T(128)}, u32[]{:S(2)}) copy-start(s32[16]{0:T(128)} %param.11) | copy-start | bytes 196
  399.9 20.7 %copy-start.8 = (s32[16]{0:T(128)S(1)}, s32[16]{0:T(128)}, u32[]{:S(2)}) copy-start(s32[16]{0:T(128)} %param.10) | copy-start | bytes 196
  399.9 21.7 %copy-start.1 = (f32[96,128]{1,0:T(8,128)S(1)}, f32[96,128]{1,0:T(8,128)}, u32[]{:S(2)}) copy-start(f32[96,128]{1,0:T(8,128)} %param.12) | copy-start | bytes 147460
where the time goes:
time: 422 us
  blocking collectives  303 us (72%)
  matrix products  45.1 us (11%)
  waiting for transfers between devices  35.7 us (8%)
  local copies, waits for them, and re-layouts  20.8 us (5%)
  other arithmetic  8.67 us (2%)
  starting transfers between devices  7.64 us (2%)
    psum x1, blocking collectives, shards(): adapter_cols = lax.psum(partial_value, 'pair').astype(jnp.bfloat16)  149 us
    psum x1, blocking collectives, shards(): grad_rounded = lax.psum(row_grad, 'pair').astype(jnp.bfloat16)  141 us
    all_to_all x1, waiting for transfers between devices, shards(): lax.all_to_all(outer_grads, 'gen', split_axis=1, concat_axis=0, tiled=True)  21.3 us
    all_to_all x1, waiting for transfers between devices, shards(): lax.all_to_all(outgoing, 'gen', split_axis=1, concat_axis=1, tiled=True)  14.3 us
    psum x1, blocking collectives, shards(): grad_pair = lax.psum(partial_pair, 'gen')  12.6 us
    dot_general x1, matrix products, shards(): jnp.dot(pair_embed, generator, preferred_element_type=jnp.float32)  10.1 us
    dot_general x1, matrix products, shards(): jnp.einsum('pe,pc->ec', pair_embed, grad_rounded, preferred_element_type=...  8.55 us
  transfers between devices with their start and end apart: 2, of which 2 were waited for; matrix products, arithmetic and copies ran while one was open for 1% of the time, Pallas kernels for 0%

commit v1 on v0

--- a/solution.py
+++ b/solution.py
@@ -29,7 +29,19 @@
     outgoing = jnp.take(adapter_cols, send_order, axis=0).reshape(
         blocks_here, gen_count * adapter_cols.shape[1]
     )
-    own_adapters = lax.all_to_all(outgoing, "gen", split_axis=1, concat_axis=1, tiled=True)
+    ways, here = (lax.axis_size("gen"), lax.axis_index("gen"))
+    width = outgoing.shape[1] // ways
+    shape = list(outgoing.shape)
+    shape[1] = width
+    height = shape[1]
+    shape[1] = height * ways
+    full = jnp.zeros(shape, outgoing.dtype)
+    for mask in range(ways):
+        part = lax.dynamic_slice_in_dim(outgoing, (here ^ mask) * width, width, axis=1)
+        if mask:
+            part = lax.ppermute(part, "gen", [(d, d ^ mask) for d in range(ways)])
+        full = lax.dynamic_update_slice_in_dim(full, part, (here ^ mask) * height, axis=1)
+    own_adapters = full
     adapters = own_adapters.reshape(blocks_here, model_width, adapter_rank)
     token_blocks = tokens.reshape(blocks_here, BLK, model_width)
     cot_blocks = cotangent.reshape(blocks_here, BLK, adapter_rank)

time: 422 us -> 450 us (1.066)
  other arithmetic: 8.67 us -> 28.4 us
  local copies, waits for them, and re-layouts: 20.8 us -> 25.7 us
    dynamic_update_slice x0 -> x1, other arithmetic: none -> 22 us  [shards(): lax.dynamic_update_slice_in_dim(full, part, (here ^ mask) * height, axis=1)]
    all_to_all x1 -> x0, waiting for transfers between devices: 14.3 us -> none  [shards(): lax.all_to_all(outgoing, 'gen', split_axis=1, concat_axis=1, tiled=True)]
    ppermute x0 -> x7, waiting for transfers between devices: none -> 13.1 us  [shards(): part = lax.ppermute(part, 'gen', [(d, d ^ mask) for d in range(ways)])]
    ppermute x0 -> x7, starting transfers between devices: none -> 7.33 us  [shards(): part = lax.ppermute(part, 'gen', [(d, d ^ mask) for d in range(ways)])]
    unnamed x1 -> x0, other arithmetic: 7.03 us -> none
    dynamic_update_slice x0 -> x7, local copies, waits for them, and re-layouts: none -> 6.75 us  [shards(): lax.dynamic_update_slice_in_dim(full, part, (here ^ mask) * height, axis=1)]
    all_to_all x1 -> x0, local copies, waits for them, and re-layouts: 5.99 us -> none  [shards(): lax.all_to_all(outgoing, 'gen', split_axis=1, concat_axis=1, tiled=True)]
    select_n x2, other arithmetic: 0.9 us -> 5.72 us  [shards(): jnp.take(adapter_cols, send_order, axis=0)]
  transfers between devices with their start and end apart: 2 -> 8, of which waited for: 2 -> 4; matrix products, arithmetic and copies ran while one was open for 1% -> 3% of each run, Pallas kernels for 0% -> 0%
where the time goes in v1:
time: 450 us
  blocking collectives  303 us (67%)
  matrix products  45.1 us (10%)
  waiting for transfers between devices  34.8 us (8%)
  other arithmetic  28.4 us (6%)
  local copies, waits for them, and re-layouts  25.7 us (6%)
  starting transfers between devices  11.7 us (3%)
    psum x1, blocking collectives, shards(): adapter_cols = lax.psum(partial_value, 'pair').astype(jnp.bfloat16)  149 us
    psum x1, blocking collectives, shards(): grad_rounded = lax.psum(row_grad, 'pair').astype(jnp.bfloat16)  141 us
    dynamic_update_slice x1, other arithmetic, shards(): lax.dynamic_update_slice_in_dim(full, part, (here ^ mask) * height, axis=1)  22 us
    all_to_all x1, waiting for transfers between devices, shards(): lax.all_to_all(outer_grads, 'gen', split_axis=1, concat_axis=0, tiled=True)  21.7 us
    ppermute x7, waiting for transfers between devices, shards(): part = lax.ppermute(part, 'gen', [(d, d ^ mask) for d in range(ways)])  13.1 us
    psum x1, blocking collectives, shards(): grad_pair = lax.psum(partial_pair, 'gen')  12.4 us
    dot_general x1, matrix products, shards(): jnp.dot(pair_embed, generator, preferred_element_type=jnp.float32)  10.1 us
  transfers between devices with their start and end apart: 8, of which 4 were waited for; matrix products, arithmetic and copies ran while one was open for 3% of the time, Pallas kernels for 0%

profile of v1, /device:TPU:0, one launch (start us, length us, event | category | flops | bytes accessed | tf_op | source)
XLA Modules:
  0.0 449.5 jit_solution(9677962106880586276)
XLA Ops:
  3.0 10.1 %fusion.21 = f32[16,65536]{1,0:T(8,128)} fusion(bf16[16,128]{1,0:T(8,128)(2,1)S(1)} %convolution_convert_fusion.2, bf16[128,65536]{1,0:T(8,128)(2,1)} %param.13), kind=kOutput, calls=%fused_computation.53 | convolution fusion | flops 268435456 | bytes 20975616 | tf_op jit(solution)/shard_map/dot_general | solution.py:22
  13.1 149.0 %all-reduce.2 = bf16[16,65536]{1,0:T(8,128)(2,1)S(1)} all-reduce(f32[16,65536]{1,0:T(8,128)} %fusion.21), channel_id=1, replica_groups=mesh['pair'=4,'gen'=8] {'pair'}, use_global_device_ids=true, to_apply=%region_0.0 | all-reduce | flops 1048576 | bytes 6291456 | tf_op jit(solution)/shard_map/psum | solution.py:23
  163.4 2.9 copy.18
  166.5 1.9 copy.17
  168.5 5.0 %broadcast_select_fusion = bf16[1,524288]{1,0:T(2,128)(2,1)S(1)} fusion(pred[1,524288]{1,0:T(4,128)(4,1)S(1)} %bitcast.33, bf16[1,524288]{1,0:T(2,128)(2,1)} %bitcast.34), kind=kLoop, calls=%fused_computation.15 | loop fusion | flops 524288 | bytes 2621440 | tf_op jit(solution)/shard_map/jit(_take)/select_n | solution.py:29
  174.6 3.1 constant_dynamic-slice_fusion
  177.7 1.5 collective-permute-start.1
  179.5 1.5 collective-permute-start.3
  182.2 2.4 collective-permute-start.5
  189.7 2.2 collective-permute-done.2
  194.4 9.7 %collective-permute-done.4 = bf16[1,65536]{1,0:T(2,128)(2,1)} collective-permute-done((bf16[1,65536]{1,0:T(2,128)(2,1)S(1)}, bf16[1,65536]{1,0:T(2,128)(2,1)}, u32[]{:S(2)}, u32[]{:S(2)}) %collective-permute-start.4) | collective-permute-done | bytes 131104 | tf_op jit(solution)/shard_map/ppermute | solution.py:42
  206.0 22.0 %reduce = bf16[524288]{0:T(1024)(128)(2,1)S(1)} reduce(bf16[1,524288]{1,0:T(2,128)(2,1)S(1)} %constant_dynamic-update-slice_fusion.6, bf16[]{:T(256)} %constant.52), dimensions={0}, to_apply=%dynamic_update_slice.31.reduce_sub_computation | reduce | bytes 2097154 | tf_op jit(solution)/shard_map/dynamic_update_slice | solution.py:43
  228.4 3.9 convolution_bitcast_fusion.1
  233.3 2.9 convolution_bitcast_fusion
  236.2 1.9 copy.14
  238.1 4.2 all_to_all.15
  242.2 4.3 all-to-all-start
  246.6 5.0 %convolution_convert_fusion.1 = bf16[1024,2048]{1,0:T(8,128)(2,1)} fusion(bf16[2048,256]{1,0:T(8,128)(2,1)S(1)} %copy-done.3, f32[1024,256]{0,1:T(8,128)} %copy-done.9, bf16[1024,256]{0,1:T(8,128)(2,1)} %copy.13), kind=kOutput, calls=%fused_computation.2 | convolution fusion | flops 1078460416 | bytes 6815744 | tf_op jit(solution)/shard_map/btr,bdr->btd/dot_general | solution.py:54
  251.6 21.7 %all-to-all-done = f32[1,8,65536]{2,0,1:T(1,128)S(1)} async-done(((f32[1,8,65536]{2,0,1:T(1,128)}), f32[1,8,65536]{2,0,1:T(1,128)S(1)}, u32[]{:S(2)}, u32[]{:S(2)}) %all-to-all-start) | async-done | bytes 2097184 | tf_op jit(solution)/shard_map/all_to_all | solution.py:61
  273.2 4.8 %fusion = f32[16,65536]{1,0:T(8,128)} fusion(f32[1,8,65536]{2,0,1:T(1,128)S(1)} %all-to-all-done, s32[8]{0:T(128)S(1)} %get-tuple-element.4), kind=kOutput, calls=%fused_computation.4 | convolution fusion | flops 100663424 | bytes 6291488 | tf_op jit(solution)/shard_map/dot_general | solution.py:64
  278.0 141.5 %all-reduce.3 = bf16[16,65536]{1,0:T(8,128)(2,1)S(1)} all-reduce(f32[16,65536]{1,0:T(8,128)} %fusion), channel_id=1, replica_groups=mesh['pair'=4,'gen'=8] {'pair'}, use_global_device_ids=true, to_apply=%region_1.2 | all-reduce | flops 1048576 | bytes 6291456 | tf_op jit(solution)/shard_map/psum | solution.py:65
  419.5 8.5 %convolution_convert_fusion = bf16[128,65536]{1,0:T(8,128)(2,1)} fusion(bf16[16,128]{1,0:T(8,128)(2,1)S(1)} %convolution_convert_fusion.2, bf16[16,65536]{1,0:T(8,128)(2,1)S(1)} %all-reduce.3), kind=kOutput, calls=%fused_computation.1 | convolution fusion | flops 276824064 | bytes 18878464 | tf_op jit(solution)/shard_map/pe,pc->ec/dot_general | solution.py:66
  428.0 8.1 %fusion.22 = f32[16,128]{1,0:T(8,128)S(1)} fusion(bf16[16,65536]{1,0:T(8,128)(2,1)S(1)} %all-reduce.3, bf16[128,65536]{1,0:T(8,128)(2,1)} %param.13), kind=kOutput, calls=%fused_computation.54 | convolution fusion | flops 268435456 | bytes 18882560 | tf_op jit(solution)/shard_map/pc,ec->pe/dot_general | solution.py:69
  436.1 12.4 %psum.23 = f32[16,128]{1,0:T(8,128)S(1)} all-reduce(f32[16,128]{1,0:T(8,128)S(1)} %fusion.22), channel_id=1, replica_groups=mesh['pair'=4,'gen'=8] {'gen'}, use_global_device_ids=true, to_apply=%region_2.3 | all-reduce | flops 2048 | bytes 16384 | tf_op jit(solution)/shard_map/psum | solution.py:72
  (46 shorter events, 18.1 us)
Async XLA Ops:
  0.6 1.5 copy-start
  174.6 6.6 %copy-start.4 = (bf16[1024,256]{1,0:T(8,128)(2,1)S(1)}, bf16[1024,256]{1,0:T(8,128)(2,1)}, u32[]{:S(2)}) copy-start(bf16[1024,256]{1,0:T(8,128)(2,1)} %param.8) | copy-start | bytes 1572868
  177.7 4.5 %collective-permute-start = (bf16[1,65536]{1,0:T(2,128)(2,1)}, bf16[1,65536]{1,0:T(2,128)(2,1)}, u32[]{:S(2)}, u32[]{:S(2)}) collective-permute-start(bf16[1,65536]{1,0:T(2,128)(2,1)} %get-tuple-element.11), channel_id=1, source_target_pairs={{0,1},{1,0},{2,3},{3,2},{4,5},{5,4},{6,7},{7,6},{8,9},{9,8},{10,11... | collective-permute-start | bytes 393224 | tf_op jit(solution)/shard_map/ppermute | solution.py:42
  177.7 9.4 %collective-permute-start.1 = (bf16[1,65536]{1,0:T(2,128)(2,1)}, bf16[1,65536]{1,0:T(2,128)(2,1)}, u32[]{:S(2)}, u32[]{:S(2)}) collective-permute-start(bf16[1,65536]{1,0:T(2,128)(2,1)} %get-tuple-element.10), channel_id=1, source_target_pairs={{0,2},{1,3},{2,0},{3,1},{4,6},{5,7},{6,4},{7,5},{8,10},{9,11},{10,... | collective-permute-start | bytes 393224 | tf_op jit(solution)/shard_map/ppermute | solution.py:42
  179.2 12.8 %collective-permute-start.2 = (bf16[1,65536]{1,0:T(2,128)(2,1)}, bf16[1,65536]{1,0:T(2,128)(2,1)}, u32[]{:S(2)}, u32[]{:S(2)}) collective-permute-start(bf16[1,65536]{1,0:T(2,128)(2,1)} %get-tuple-element.9), channel_id=1, source_target_pairs={{0,3},{1,2},{2,1},{3,0},{4,7},{5,6},{6,5},{7,4},{8,11},{9,10},{10,... | collective-permute-start | bytes 393224 | tf_op jit(solution)/shard_map/ppermute | solution.py:42
  179.5 13.6 %collective-permute-start.3 = (bf16[1,65536]{1,0:T(2,128)(2,1)}, bf16[1,65536]{1,0:T(2,128)(2,1)}, u32[]{:S(2)}, u32[]{:S(2)}) collective-permute-start(bf16[1,65536]{1,0:T(2,128)(2,1)} %get-tuple-element.8), channel_id=1, source_target_pairs={{0,4},{1,5},{2,6},{3,7},{4,0},{5,1},{6,2},{7,3},{8,12},{9,13},{10,... | collective-permute-start | bytes 393224 | tf_op jit(solution)/shard_map/ppermute | solution.py:42
  181.1 23.1 %collective-permute-start.4 = (bf16[1,65536]{1,0:T(2,128)(2,1)S(1)}, bf16[1,65536]{1,0:T(2,128)(2,1)}, u32[]{:S(2)}, u32[]{:S(2)}) collective-permute-start(bf16[1,65536]{1,0:T(2,128)(2,1)S(1)} %get-tuple-element.7), channel_id=1, source_target_pairs={{0,5},{1,4},{2,7},{3,6},{4,1},{5,0},{6,3},{7,2},{8,13},{9,12},{10,... | collective-permute-start | bytes 393224 | tf_op jit(solution)/shard_map/ppermute | solution.py:42
  182.2 23.2 %collective-permute-start.5 = (bf16[1,65536]{1,0:T(2,128)(2,1)S(1)}, bf16[1,65536]{1,0:T(2,128)(2,1)S(1)}, u32[]{:S(2)}, u32[]{:S(2)}) collective-permute-start(bf16[1,65536]{1,0:T(2,128)(2,1)S(1)} %get-tuple-element.6), channel_id=1, source_target_pairs={{0,6},{1,7},{2,4},{3,5},{4,2},{5,3},{6,0},{7,1},{8,14},{9,15},{10,... | collective-permute-start | bytes 393224 | tf_op jit(solution)/shard_map/ppermute | solution.py:42
  187.1 18.6 %collective-permute-start.6 = (bf16[1,65536]{1,0:T(2,128)(2,1)S(1)}, bf16[1,65536]{1,0:T(2,128)(2,1)S(1)}, u32[]{:S(2)}, u32[]{:S(2)}) collective-permute-start(bf16[1,65536]{1,0:T(2,128)(2,1)S(1)} %get-tuple-element.5), channel_id=1, source_target_pairs={{0,7},{1,6},{2,5},{3,4},{4,3},{5,2},{6,1},{7,0},{8,15},{9,14},{10,... | collective-permute-start | bytes 393224 | tf_op jit(solution)/shard_map/ppermute | solution.py:42
  228.4 3.9 copy-start.2
  228.4 4.9 %copy-start.5 = (bf16[1024,256]{0,1:T(8,128)(2,1)S(1)}, bf16[1024,256]{0,1:T(8,128)(2,1)}, u32[]{:S(2)}) copy-start(bf16[1024,256]{0,1:T(8,128)(2,1)} %copy.13) | copy-start | bytes 1572868
  228.4 4.9 %copy-start.6 = (bf16[1024,2048]{1,0:T(8,128)(2,1)S(1)}, bf16[1024,2048]{1,0:T(8,128)(2,1)}, u32[]{:S(2)}) copy-start(bf16[1024,2048]{1,0:T(8,128)(2,1)} %param.7) | copy-start | bytes 12582916
  232.3 1.0 copy-start.9
  242.2 4.3 copy-start.3
  242.2 31.0 %all-to-all-start = ((f32[1,8,65536]{2,0,1:T(1,128)}), f32[1,8,65536]{2,0,1:T(1,128)S(1)}, u32[]{:S(2)}, u32[]{:S(2)}) async-start(f32[1,8,65536]{2,0,1:T(1,128)} %all_to_all.15), calls=%async_computation | async-start | bytes 4194304 | tf_op jit(solution)/shard_map/all_to_all | solution.py:61
  428.0 20.5 %copy-start.7 = (s32[16]{0:T(128)S(1)}, s32[16]{0:T(128)}, u32[]{:S(2)}) copy-start(s32[16]{0:T(128)} %param.11) | copy-start | bytes 196
  428.0 20.5 %copy-start.8 = (s32[16]{0:T(128)S(1)}, s32[16]{0:T(128)}, u32[]{:S(2)}) copy-start(s32[16]{0:T(128)} %param.10) | copy-start | bytes 196
  428.0 21.5 %copy-start.1 = (f32[96,128]{1,0:T(8,128)S(1)}, f32[96,128]{1,0:T(8,128)}, u32[]{:S(2)}) copy-start(f32[96,128]{1,0:T(8,128)} %param.12) | copy-start | bytes 147460
